TPU v7x, 32 devices: a whole 2x2x4 slice. The times are simulated.
32 devices in a mesh: blk: 8 (over z, y), dp: 4 (over x, core).
Axes of the slice: x: 2, y: 2, z: 4, core: 2. Of those that a mesh axis runs over, the one named last changes fastest.
Arguments:
- feature_map: bfloat16 [20480, 320], P(('blk', 'dp')), may hold values from -8 to 8, as said below
- head_weight: bfloat16 [320, 1280], replicated, may hold values from -0.3125 to 0.3125
- head_shift: float32 [1280], replicated, may hold values from -0.5 to 0.5
- proj_weight: bfloat16 [1280, 256], replicated, may hold values from -0.15625 to 0.15625
Outputs:
- loss: float32 [], replicated
- grad_head: float32 [320, 1280], replicated
- grad_shift: float32 [1280], replicated
- grad_proj: float32 [1280, 256], replicated
Inputs may be any that keep to these rules, and one draw needn't show every extreme that they name: `feature_map`: features of order one.
All inputs are finite; a program needn't handle non-finite values.
Results may differ from a plain program's by a relative error of at most 0.00067.
Values may be sent and summed in bfloat16 or wider, within the bound.
No kernel may reach another device: no remote copies, remote signals or barrier semaphores. Data moves between devices by JAX's collectives and lax.ppermute only.
A program may use at most 64 MiB of HBM per device.

v0:
```python
import jax
import jax.numpy as jnp
from jax import lax
from jax.sharding import PartitionSpec as P

POS = 16


def pair_terms(rows_z, row_ids, piece, col_ids):
    sim = lax.dot_general(
        rows_z, piece, (((1,), (1,)), ((), ())), preferred_element_type=jnp.float32
    )
    kern = jnp.exp(4.0 * (sim - 1.0))
    kern = jnp.where(row_ids[:, None] == col_ids[None, :], jnp.float32(0.0), kern)
    srow = jnp.sum(kern, axis=1)
    numer = jnp.dot(kern.astype(jnp.bfloat16), piece, preferred_element_type=jnp.float32)
    return (srow, numer)


def body(feature_map, head_weight, head_shift, proj_weight):
    images = feature_map.shape[0] // POS
    channels = head_weight.shape[1]
    pre = jnp.dot(feature_map, head_weight, preferred_element_type=jnp.float32) + head_shift
    act = jax.nn.silu(pre)
    pooled = jnp.mean(act.reshape(images, POS, channels), axis=1).astype(jnp.bfloat16)
    proj = jnp.dot(pooled, proj_weight, preferred_element_type=jnp.float32)
    rnorm = jnp.sqrt(jnp.sum(proj * proj, axis=1, keepdims=True) + 1e-06)
    unit = proj / rnorm
    zed = unit.astype(jnp.bfloat16)
    batch = images * lax.axis_size("blk") * lax.axis_size("dp")
    my_ids = lax.axis_index(("blk", "dp")) * images + jnp.arange(images, dtype=jnp.int32)
    piece = lax.all_gather(zed, ("blk", "dp"), axis=0, tiled=True)
    col_ids = jnp.arange(piece.shape[0], dtype=jnp.int32)
    srow, numer = pair_terms(zed, my_ids, piece, col_ids)
    total = lax.psum(jnp.sum(srow), ("blk", "dp"))
    loss = jnp.log(total / (batch * (batch - 1.0)))
    grad_unit = batch * 8.0 / total * numer
    grad_rows = (
        (grad_unit - unit * jnp.sum(unit * grad_unit, axis=1, keepdims=True)) / rnorm
    ).astype(jnp.bfloat16)
    grad_proj = lax.dot_general(
        pooled, grad_rows, (((0,), (0,)), ((), ())), preferred_element_type=jnp.float32
    )
    grad_pooled = lax.dot_general(
        grad_rows, proj_weight, (((1,), (1,)), ((), ())), preferred_element_type=jnp.float32
    )
    grad_act = jnp.broadcast_to((grad_pooled / POS)[:, None, :], (images, POS, channels)).reshape(
        images * POS, channels
    )
    sig = jax.nn.sigmoid(pre)
    grad_pre = (grad_act * sig * (1.0 + pre * (1.0 - sig))).astype(jnp.bfloat16)
    grad_shift = jnp.sum(grad_pre.astype(jnp.float32), axis=0)
    grad_head = lax.dot_general(
        feature_map, grad_pre, (((0,), (0,)), ((), ())), preferred_element_type=jnp.float32
    )
    grad_head, grad_shift, grad_proj = lax.psum((grad_head, grad_shift, grad_proj), ("blk", "dp"))
    return (loss, grad_head, grad_shift, grad_proj)


def solution(mesh):
    return jax.shard_map(
        body,
        mesh=mesh,
        in_specs=(P(("blk", "dp"), None), P(), P(), P()),
        out_specs=(P(), P(), P(), P()),
        check_vma=False,
    )
```

profile of v0, /device:TPU:0, one launch (start us, length us, event | category | flops | bytes accessed | tf_op | source)
XLA Modules:
  0.0 256.1 jit_solution(15273268031777491178)
XLA Ops:
  7.2 0.0 copy-start
  7.2 0.0 all-reduce.3.cloned.1.call-start
  7.2 1.1 copy-done
  8.3 5.0 %fusion.2 = (f32[640,1280]{1,0:T(8,128)}, f32[640,1280]{1,0:T(8,128)}) fusion(f32[1280]{0:T(1024)} %param.6, bf16[640,320]{0,1:T(8,128)(2,1)} %param.4, bf16[320,1280]{1,0:T(8,128)(2,1)S(1)} %copy-done), kind=kOutput, calls=%fused_computation.6 | convolution fusion | flops 528384000 | bytes 7787520 | tf_op jit(solution)/shard_map/dot_general | solution.py:23
  13.3 0.0 copy-start.2
  13.3 2.5 reduce_sum.49
  15.8 0.0 copy-done.2
  15.8 0.3 multiply_reduce_fusion.1
  16.2 0.1 fusion.11
  16.3 45.0 %all_gather.3 = bf16[1280,256]{1,0:T(8,128)(2,1)S(1)} all-gather(bf16[40,256]{1,0:T(8,128)(2,1)S(1)} %fusion.11), channel_id=1, replica_groups=mesh['blk'=8,'dp'=4] {'blk','dp'}, dimensions={0}, use_global_device_ids=true | all-gather | bytes 675840 | tf_op jit(solution)/shard_map/all_gather | solution.py:32
  61.3 1.0 fusion.13
  62.3 37.0 %psum.28 = f32[]{:T(128)} all-reduce(f32[]{:T(128)} %get-tuple-element.12), channel_id=1, replica_groups=mesh['blk'=8,'dp'=4] {'blk','dp'}, use_global_device_ids=true, to_apply=%region_3.4 | all-reduce | flops 1 | bytes 8 | tf_op jit(solution)/shard_map/psum | solution.py:35
  100.0 0.0 copy-start.1
  100.0 0.3 multiply_reduce_fusion
  100.4 1.5 fusion.7
  101.8 0.0 copy-start.4
  101.8 0.4 convolution_multiply_fusion
  102.2 0.2 copy-done.1
  102.4 1.4 convert_reduce_fusion
  103.7 0.0 copy-done.4
  103.8 2.0 convolution_bitcast_fusion
  105.7 0.0 all-reduce.3.cloned.1.call-update
  106.4 41.6 %psum.30 = f32[1280]{0:T(1024)} all-reduce(f32[1280]{0:T(1024)S(1)} %get-tuple-element.6), channel_id=1, replica_groups=mesh['blk'=8,'dp'=4] {'blk','dp'}, use_global_device_ids=true, to_apply=%region_7.8 | all-reduce | flops 1280 | bytes 10240 | tf_op jit(solution)/shard_map/psum | solution.py:56
  148.0 96.3 %all-reduce.3.cloned.1.call-done = (f32[320,1280]{1,0:T(8,128)}, f32[1280,256]{1,0:T(8,128)}) async-done(((f32[320,1280]{1,0:T(8,128)}, f32[1280,256]{1,0:T(8,128)}), (f32[320,1280]{1,0:T(8,128)}, f32[1280,256]{1,0:T(8,128)})) %all-reduce.3.cloned.1.call-update) | async-done | bytes 2949136 | tf_op jit(solution)/shard_map/psum | solution.py:56
  244.3 0.0 copy-start.3
  244.3 2.8 %copy.10 = f32[320,1280]{1,0:T(8,128)} copy(f32[320,1280]{1,0:T(8,128)} %get-tuple-element.19) | data formatting | bytes 3276800
  247.1 0.0 copy-done.3
  247.1 1.1 copy.11
  (2 shorter events, 0.0 us)
Async XLA Ops:
  7.2 1.2 copy-start
  7.2 237.1 %all-reduce.3.cloned.1.call-start = ((), (), s32[]{:S(2)}) async-start(), calls=%async_computation | async-start | bytes 5898240 | tf_op jit(solution)/shard_map/psum | solution.py:56
  13.3 2.5 copy-start.2
  100.0 2.4 copy-start.1
  101.8 1.9 copy-start.4
  244.3 2.8 %copy-start.3 = (f32[1280,256]{1,0:T(8,128)S(1)}, f32[1280,256]{1,0:T(8,128)}, u32[]{:S(2)}) copy-start(f32[1280,256]{1,0:T(8,128)} %get-tuple-element.21) | copy-start | bytes 3932164
Sparse Core Ops, SparseCore 0:
  105.9 138.3 all-reduce.2
where the time goes:
time: 257 us; the launch traced here: 256 us
  blocking collectives  124 us (48%)
  waiting for transfers between devices  96.3 us (37%)
  between operations  16.6 us (6%)
  matrix products  10.4 us (4%)
  local copies, waits for them, and re-layouts  5.18 us (2%)
  other arithmetic  3.97 us (2%)
    psum x1, waiting for transfers between devices, body(): lax.psum((grad_head, grad_shift, grad_proj), ('blk', 'dp'))  96.3 us
    all_gather x1, blocking collectives, body(): piece = lax.all_gather(zed, ('blk', 'dp'), axis=0, tiled=True)  45 us
    psum x1, blocking collectives, body(): lax.psum((grad_head, grad_shift, grad_proj), ('blk', 'dp'))  41.6 us
    psum x1, blocking collectives, body(): total = lax.psum(jnp.sum(srow), ('blk', 'dp'))  37 us
    unnamed x12, local copies, waits for them, and re-layouts  5.18 us
  transfers between devices with their start and end apart: 1, of which 1 were waited for; matrix products, arithmetic and copies ran while one was open for 0% of the time, Pallas kernels for 0%

commit v1 on v0

--- a/solution.py
+++ b/solution.py
@@ -4,6 +4,23 @@
 from jax.sharding import PartitionSpec as P
 
 POS = 16
+
+
+def joined_along(tiles, dim):
+    tiles = jnp.moveaxis(tiles, 0, dim)
+    shape = tiles.shape
+    return tiles.reshape(*shape[:dim], shape[dim] * shape[dim + 1], *shape[dim + 2 :])
+
+
+def doubled(value, axis):
+    size, position = (lax.axis_size(axis), lax.axis_index(axis))
+    pieces, bit = (value[None], 1)
+    while bit < size:
+        other = lax.ppermute(pieces, axis, [(i, i ^ bit) for i in range(size)])
+        low = position & bit == 0
+        pieces = jnp.concatenate([jnp.where(low, pieces, other), jnp.where(low, other, pieces)])
+        bit *= 2
+    return pieces
 
 
 def pair_terms(rows_z, row_ids, piece, col_ids):
@@ -29,7 +46,7 @@
     zed = unit.astype(jnp.bfloat16)
     batch = images * lax.axis_size("blk") * lax.axis_size("dp")
     my_ids = lax.axis_index(("blk", "dp")) * images + jnp.arange(images, dtype=jnp.int32)
-    piece = lax.all_gather(zed, ("blk", "dp"), axis=0, tiled=True)
+    piece = joined_along(doubled(zed, ("blk", "dp")), 0)
     col_ids = jnp.arange(piece.shape[0], dtype=jnp.int32)
     srow, numer = pair_terms(zed, my_ids, piece, col_ids)
     total = lax.psum(jnp.sum(srow), ("blk", "dp"))

time: 257 us -> 246 us (0.957)
  blocking collectives: 124 us -> 81.4 us
  waiting for transfers between devices: 96.3 us -> 116 us
  starting transfers between devices: 0.04 us -> 11.5 us
    all_gather x1 -> x0, blocking collectives: 45 us -> none  [body(): piece = lax.all_gather(zed, ('blk', 'dp'), axis=0, tiled=True)]
    ppermute x0 -> x5, waiting for transfers between devices: none -> 19.5 us  [doubled(): other = lax.ppermute(pieces, axis, [(i, i ^ bit) for i in range(size)])]
    ppermute x0 -> x5, starting transfers between devices: none -> 11.5 us  [doubled(): other = lax.ppermute(pieces, axis, [(i, i ^ bit) for i in range(size)])]
    psum x1, blocking collectives: 37 us -> 40 us  [body(): total = lax.psum(jnp.sum(srow), ('blk', 'dp'))]
  transfers between devices with their start and end apart: 1 -> 6, of which waited for: 1 -> 6; matrix products, arithmetic and copies ran while one was open for 0% -> 0% of each run, Pallas kernels for 0% -> 0%
where the time goes in v1:
time: 246 us; the launch traced here: 245 us
  waiting for transfers between devices  116 us (47%)
  blocking collectives  81.4 us (33%)
  between operations  16.7 us (7%)
  starting transfers between devices  11.5 us (5%)
  matrix products  10.4 us (4%)
  local copies, waits for them, and re-layouts  5.19 us (2%)
  other arithmetic  4.29 us (2%)
    psum x1, waiting for transfers between devices, body(): lax.psum((grad_head, grad_shift, grad_proj), ('blk', 'dp'))  96.2 us
    psum x1, blocking collectives, body(): lax.psum((grad_head, grad_shift, grad_proj), ('blk', 'dp'))  41.4 us
    psum x1, blocking collectives, body(): total = lax.psum(jnp.sum(srow), ('blk', 'dp'))  40 us
    ppermute x5, waiting for transfers between devices, doubled(): other = lax.ppermute(pieces, axis, [(i, i ^ bit) for i in range(size)])  19.5 us
    ppermute x5, starting transfers between devices, doubled(): other = lax.ppermute(pieces, axis, [(i, i ^ bit) for i in range(size)])  11.5 us
    unnamed x12, local copies, waits for them, and re-layouts  5.19 us
    dot_general x1, matrix products, body(): jnp.dot(feature_map, head_weight, preferred_element_type=jnp.float32)  4.98 us
  transfers between devices with their start and end apart: 6, of which 6 were waited for; matrix products, arithmetic and copies ran while one was open for 0% of the time, Pallas kernels for 0%

profile of v1, /device:TPU:0, one launch (start us, length us, event | category | flops | bytes accessed | tf_op | source)
XLA Modules:
  0.0 245.2 jit_solution(12267625093980262779)
XLA Ops:
  7.2 0.0 copy-start
  7.2 0.0 all-reduce.3.cloned.1.call-start
  7.2 1.1 copy-done
  8.3 5.0 %fusion.2 = (f32[640,1280]{1,0:T(8,128)}, f32[640,1280]{1,0:T(8,128)}) fusion(f32[1280]{0:T(1024)} %param.6, bf16[640,320]{0,1:T(8,128)(2,1)} %param.4, bf16[320,1280]{1,0:T(8,128)(2,1)S(1)} %copy-done), kind=kOutput, calls=%fused_computation.6 | convolution fusion | flops 528384000 | bytes 7787520 | tf_op jit(solution)/shard_map/dot_general | solution.py:40
  13.3 0.0 copy-start.2
  13.3 2.5 %reduce_sum.49 = f32[40,1280]{1,0:T(8,128)S(1)} reduce(f32[40,16,1280]{2,1,0:T(8,128)} %bitcast.24, f32[]{:T(128)} %constant.12.clone.1), dimensions={1}, to_apply=%region_0.1 | reduce | flops 768000 | bytes 3481604 | tf_op jit(solution)/shard_map/reduce_sum | solution.py:42
  15.8 0.0 copy-done.2
  15.8 0.3 multiply_reduce_fusion.1
  16.2 0.1 convert_bitcast_fusion
  16.3 0.6 collective-permute-start
  16.8 0.8 collective-permute-done
  17.7 0.1 broadcast_select_fusion.9
  17.8 2.9 %collective-permute-start.1 = (bf16[2,40,256]{2,1,0:T(8,128)(2,1)S(1)}, bf16[2,40,256]{2,1,0:T(8,128)(2,1)S(1)}, u32[]{:S(2)}, u32[]{:S(2)}) collective-permute-start(bf16[2,40,256]{2,1,0:T(8,128)(2,1)S(1)} %pad_maximum_fusion.4), channel_id=1, source_target_pairs={{0,2},{1,3},{2,0},{3,1},{4,6},{5,7},{6,4},{7,5},{8,10},{9,11},{10,... | collective-permute-start | bytes 122888 | tf_op jit(solution)/shard_map/ppermute | solution.py:19
  20.7 2.0 collective-permute-done.1
  22.7 2.1 collective-permute-start.2
  24.8 2.4 collective-permute-done.2
  27.3 2.1 collective-permute-start.3
  29.4 3.3 %collective-permute-done.3 = bf16[8,40,256]{2,1,0:T(8,128)(2,1)S(1)} collective-permute-done((bf16[8,40,256]{2,1,0:T(8,128)(2,1)S(1)}, bf16[8,40,256]{2,1,0:T(8,128)(2,1)S(1)}, u32[]{:S(2)}, u32[]{:S(2)}) %collective-permute-start.3) | collective-permute-done | bytes 163872 | tf_op jit(solution)/shard_map/ppermute | solution.py:19
  32.8 3.8 %collective-permute-start.4 = (bf16[16,40,256]{2,1,0:T(8,128)(2,1)S(1)}, bf16[16,40,256]{2,1,0:T(8,128)(2,1)S(1)}, u32[]{:S(2)}, u32[]{:S(2)}) collective-permute-start(bf16[16,40,256]{2,1,0:T(8,128)(2,1)S(1)} %pad_maximum_fusion.1), channel_id=1, source_target_pairs={{0,16},{1,17},{2,18},{3,19},{4,20},{5,21},{6,22},{7,23},{8,24},{9,... | collective-permute-start | bytes 983048 | tf_op jit(solution)/shard_map/ppermute | solution.py:19
  36.5 10.9 %collective-permute-done.4 = bf16[16,40,256]{2,1,0:T(8,128)(2,1)S(1)} collective-permute-done((bf16[16,40,256]{2,1,0:T(8,128)(2,1)S(1)}, bf16[16,40,256]{2,1,0:T(8,128)(2,1)S(1)}, u32[]{:S(2)}, u32[]{:S(2)}) %collective-permute-start.4) | collective-permute-done | bytes 327712 | tf_op jit(solution)/shard_map/ppermute | solution.py:19
  47.5 0.1 pad_maximum_fusion
  47.6 1.0 fusion.13
  48.6 40.0 %psum.28 = f32[]{:T(128)} all-reduce(f32[]{:T(128)} %get-tuple-element.22), channel_id=1, replica_groups=mesh['blk'=8,'dp'=4] {'blk','dp'}, use_global_device_ids=true, to_apply=%region_3.4 | all-reduce | flops 1 | bytes 8 | tf_op jit(solution)/shard_map/psum | solution.py:52
  89.3 0.0 copy-start.1
  89.3 0.3 multiply_reduce_fusion
  89.6 1.5 fusion.7
  91.1 0.0 copy-start.4
  91.1 0.4 convolution_multiply_fusion
  91.4 0.2 copy-done.1
  91.7 1.4 convert_reduce_fusion
  93.0 0.0 copy-done.4
  93.0 2.0 convolution_bitcast_fusion
  95.0 0.0 all-reduce.3.cloned.1.call-update
  95.7 41.4 %psum.30 = f32[1280]{0:T(1024)} all-reduce(f32[1280]{0:T(1024)S(1)} %get-tuple-element.6), channel_id=1, replica_groups=mesh['blk'=8,'dp'=4] {'blk','dp'}, use_global_device_ids=true, to_apply=%region_7.8 | all-reduce | flops 1280 | bytes 10240 | tf_op jit(solution)/shard_map/psum | solution.py:73
  137.1 96.2 %all-reduce.3.cloned.1.call-done = (f32[320,1280]{1,0:T(8,128)}, f32[1280,256]{1,0:T(8,128)}) async-done(((f32[320,1280]{1,0:T(8,128)}, f32[1280,256]{1,0:T(8,128)}), (f32[320,1280]{1,0:T(8,128)}, f32[1280,256]{1,0:T(8,128)})) %all-reduce.3.cloned.1.call-update) | async-done | bytes 2949136 | tf_op jit(solution)/shard_map/psum | solution.py:73
  233.3 0.0 copy-start.3
  233.3 2.8 %copy.10 = f32[320,1280]{1,0:T(8,128)} copy(f32[320,1280]{1,0:T(8,128)} %get-tuple-element.29) | data formatting | bytes 3276800
  236.1 0.0 copy-done.3
  236.1 1.1 copy.11
  (10 shorter events, 0.2 us)
Async XLA Ops:
  7.2 1.2 copy-start
  7.2 226.2 %all-reduce.3.cloned.1.call-start = ((), (), s32[]{:S(2)}) async-start(), calls=%async_computation | async-start | bytes 5898240 | tf_op jit(solution)/shard_map/psum | solution.py:73
  13.3 2.5 %copy-start.2 = (bf16[1280,256]{1,0:T(8,128)(2,1)S(1)}, bf16[1280,256]{1,0:T(8,128)(2,1)}, u32[]{:S(2)}) copy-start(bf16[1280,256]{1,0:T(8,128)(2,1)} %param.7) | copy-start | bytes 1966084
  16.3 1.4 collective-permute-start
  17.8 4.9 %collective-permute-start.1 = (bf16[2,40,256]{2,1,0:T(8,128)(2,1)S(1)}, bf16[2,40,256]{2,1,0:T(8,128)(2,1)S(1)}, u32[]{:S(2)}, u32[]{:S(2)}) collective-permute-start(bf16[2,40,256]{2,1,0:T(8,128)(2,1)S(1)} %pad_maximum_fusion.4), channel_id=1, source_target_pairs={{0,2},{1,3},{2,0},{3,1},{4,6},{5,7},{6,4},{7,5},{8,10},{9,11},{10,... | collective-permute-start | bytes 122888 | tf_op jit(solution)/shard_map/ppermute | solution.py:19
  22.7 4.5 %collective-permute-start.2 = (bf16[4,40,256]{2,1,0:T(8,128)(2,1)S(1)}, bf16[4,40,256]{2,1,0:T(8,128)(2,1)S(1)}, u32[]{:S(2)}, u32[]{:S(2)}) collective-permute-start(bf16[4,40,256]{2,1,0:T(8,128)(2,1)S(1)} %pad_maximum_fusion.3), channel_id=1, source_target_pairs={{0,4},{1,5},{2,6},{3,7},{4,0},{5,1},{6,2},{7,3},{8,12},{9,13},{10,... | collective-permute-start | bytes 245768 | tf_op jit(solution)/shard_map/ppermute | solution.py:19
  27.3 5.4 %collective-permute-start.3 = (bf16[8,40,256]{2,1,0:T(8,128)(2,1)S(1)}, bf16[8,40,256]{2,1,0:T(8,128)(2,1)S(1)}, u32[]{:S(2)}, u32[]{:S(2)}) collective-permute-start(bf16[8,40,256]{2,1,0:T(8,128)(2,1)S(1)} %pad_maximum_fusion.2), channel_id=1, source_target_pairs={{0,8},{1,9},{2,10},{3,11},{4,12},{5,13},{6,14},{7,15},{8,0},{9,1},... | collective-permute-start | bytes 491528 | tf_op jit(solution)/shard_map/ppermute | solution.py:19
  32.8 14.7 %collective-permute-start.4 = (bf16[16,40,256]{2,1,0:T(8,128)(2,1)S(1)}, bf16[16,40,256]{2,1,0:T(8,128)(2,1)S(1)}, u32[]{:S(2)}, u32[]{:S(2)}) collective-permute-start(bf16[16,40,256]{2,1,0:T(8,128)(2,1)S(1)} %pad_maximum_fusion.1), channel_id=1, source_target_pairs={{0,16},{1,17},{2,18},{3,19},{4,20},{5,21},{6,22},{7,23},{8,24},{9,... | collective-permute-start | bytes 983048 | tf_op jit(solution)/shard_map/ppermute | solution.py:19
  89.3 2.4 copy-start.1
  91.1 1.9 copy-start.4
  233.3 2.8 %copy-start.3 = (f32[1280,256]{1,0:T(8,128)S(1)}, f32[1280,256]{1,0:T(8,128)}, u32[]{:S(2)}) copy-start(f32[1280,256]{1,0:T(8,128)} %get-tuple-element.31) | copy-start | bytes 3932164
Sparse Core Ops, SparseCore 0:
  95.1 138.1 all-reduce.2
